TPU v7x, 128 devices: a whole 4x4x4 slice. The times are simulated.
128 devices in a mesh: req: 32 (over x, z, core), tp: 4 (over y).
Axes of the slice: x: 4, y: 4, z: 4, core: 2. Of those that a mesh axis runs over, the one named last changes fastest.
Arguments:
- hidden: bfloat16 [8192, 2048], P('req', 'tp'), may hold values from -45 to 45
- routes: int32 [8192, 2], P('req'), may hold values from 0 to 7, all different within a row; in each aligned block of 256 rows (0 to 255, 256 to 511, ...) at most 128 rows name the same one
- route_weights: float32 [8192, 2], P('req'), may hold values from 0.2 to 1
- pre_gain: float32 [2048], replicated, may hold values from 0.1 to 1.9
- out_gain: float32 [2048], P('tp'), may hold values from 0.1 to 1.9
- gate_weight: bfloat16 [32, 2048, 5632], P('req', None, 'tp'), as said below
- up_weight: bfloat16 [32, 2048, 5632], P('req', None, 'tp'), as said below
- down_weight: bfloat16 [32, 5632, 2048], P('req', 'tp'), as said below
Outputs:
- residual_out: bfloat16 [8192, 2048], P('req', 'tp')
- normed_out: bfloat16 [8192, 2048], P('req', 'tp')
Inputs may be any that keep to these rules, and one draw needn't show every extreme that they name: `routes`: each row names 2 different experts; in the rows of one index of req no expert is named by more than 128 rows, a bound that some block reaches. `gate_weight`: index r holds expert r % 8. `up_weight`: index r holds expert r % 8. `down_weight`: index r holds expert r % 8.
All inputs are finite; a program needn't handle non-finite values.
Results may differ from a plain program's by a relative error of at most 0.007.
Values may be sent and summed in bfloat16 or wider, within the bound.
No kernel may reach another device: no remote copies, remote signals or barrier semaphores. Data moves between devices by JAX's collectives and lax.ppermute only.
A program may use at most 128 MiB of HBM per device.

v0:
```python
import jax
import jax.numpy as jnp
from jax import lax
from jax.sharding import PartitionSpec as P

E = 8
CAP = 128
epsilon = 1e-05


def shards(hidden, routes, route_weights, pre_gain, out_gain, gate_weight, up_weight, down_weight):
    row_count, col_part = hidden.shape
    tp_count = lax.axis_size("tp")
    req_count = lax.axis_size("req")
    full_width = col_part * tp_count
    copies = req_count // E
    slot_count = CAP // copies
    stream = hidden.astype(jnp.float32)
    whole_rows = lax.all_gather(hidden, "tp", axis=1, tiled=True).astype(jnp.float32)
    meansq = jnp.sum(whole_rows * whole_rows, axis=1) / full_width
    normed_in = (whole_rows * lax.rsqrt(meansq + epsilon)[:, None] * pre_gain[None, :]).astype(
        jnp.bfloat16
    )
    send_cols = normed_in.shape[1]
    chosen = routes.reshape(-1)
    onehot = (chosen[:, None] == jnp.arange(E, dtype=jnp.int32)[None, :]).astype(jnp.int32)
    slot_rank = jnp.sum((jnp.cumsum(onehot, axis=0) - 1) * onehot, axis=1)
    position = chosen * CAP + slot_rank
    entry_rows = jnp.arange(chosen.shape[0], dtype=jnp.int32) // routes.shape[1]
    slot_row = jnp.zeros((E * CAP,), jnp.int32).at[position].set(entry_rows)
    slot_live = jnp.zeros((E * CAP,), jnp.bool_).at[position].set(True)
    outgoing = jnp.where(slot_live[:, None], normed_in[slot_row], jnp.zeros((), jnp.bfloat16))
    outgoing = outgoing.reshape(E, slot_count, copies, send_cols).transpose(2, 0, 1, 3)
    outgoing = outgoing.reshape(req_count, slot_count, send_cols)
    pieces = lax.all_to_all(outgoing, "req", split_axis=0, concat_axis=0, tiled=True)
    sources, items, widths = pieces.shape
    flat_rows = pieces.reshape(sources * items, widths)
    gate_val = jnp.dot(flat_rows, gate_weight[0], preferred_element_type=jnp.float32)
    up_val = jnp.dot(flat_rows, up_weight[0], preferred_element_type=jnp.float32)
    activ = (jax.nn.silu(gate_val) * up_val).astype(jnp.bfloat16)
    partial_out = jnp.dot(activ, down_weight[0], preferred_element_type=jnp.float32)
    partial_out = lax.optimization_barrier(partial_out.astype(jnp.bfloat16)).astype(jnp.float32)
    summed = lax.psum_scatter(
        partial_out.reshape(sources, items, widths).astype(jnp.bfloat16),
        "tp",
        scatter_dimension=2,
        tiled=True,
    )
    returned = lax.all_to_all(summed, "req", split_axis=0, concat_axis=0, tiled=True)
    returned = returned.reshape(copies, E, slot_count, col_part).transpose(1, 2, 0, 3)
    returned = returned.reshape(E * CAP, col_part)
    picked = returned[position].reshape(row_count, routes.shape[1], col_part).astype(jnp.float32)
    mixed = jnp.sum(picked * route_weights[:, :, None], axis=1)
    total_stream = stream + mixed
    out_sums = lax.psum(jnp.sum(total_stream * total_stream, axis=1), "tp")
    normed_out = (
        total_stream * lax.rsqrt(out_sums / full_width + epsilon)[:, None] * out_gain[None, :]
    )
    return (total_stream.astype(jnp.bfloat16), normed_out.astype(jnp.bfloat16))


def solution(mesh):
    return jax.shard_map(
        shards,
        mesh=mesh,
        in_specs=(
            P("req", "tp"),
            P("req", None),
            P("req", None),
            P(),
            P("tp"),
            P("req", None, "tp"),
            P("req", None, "tp"),
            P("req", "tp", None),
        ),
        out_specs=(P("req", "tp"), P("req", "tp")),
        check_vma=False,
    )
```

profile of v0, /device:TPU:0, one launch (start us, length us, event | category | flops | bytes accessed | tf_op | source)
XLA Modules:
  0.0 241.1 jit_solution(10688515270769743538)
XLA Ops:
  7.2 0.7 all-gather.2.cloned.1.call-update
  7.9 0.8 copy.13
  9.1 1.1 reduce-window.6
  10.5 0.7 broadcast_multiply_fusion
  11.6 2.4 %scatter_custom_fusion.1 = s32[1024]{0:T(1024)S(1)} fusion(s32[512]{0:T(512)S(1)} %bitcast.42, s32[512]{0:T(512)S(1)} %add_select_fusion, s32[]{:T(128)} %constant.37.clone.1), kind=kCustom, calls=%fused_computation.41 | custom fusion | bytes 4100 | tf_op jit(solution)/shard_map/scatter | solution.py:30
  14.0 2.4 %scatter_custom_fusion = pred[1024]{0:T(1024)(128)(4,1)S(1)} fusion(s32[512]{0:T(512)S(1)} %bitcast.43, pred[512]{0:T(512)(128)(4,1)S(1)} %broadcast.99, pred[]{:T(512)} %constant.20.clone.1), kind=kCustom, calls=%fused_computation.44 | custom fusion | bytes 1025 | tf_op jit(solution)/shard_map/scatter | solution.py:31
  16.8 19.4 %all-gather.2.cloned.1.call-done = bf16[256,2048]{1,0:T(8,128)(2,1)} async-done(((bf16[256,512]{1,0:T(8,128)(2,1)}), bf16[256,2048]{1,0:T(8,128)(2,1)}) %all-gather.2.cloned.1.call-update) | async-done | bytes 1048592 | tf_op jit(solution)/shard_map/all_gather | solution.py:19
  36.1 1.5 fusion.16
  37.7 1.5 fusion.18
  39.2 6.0 %gather_fusion = bf16[1024,2048]{1,0:T(8,128)(2,1)} fusion(bf16[256,2048]{1,0:T(8,128)(2,1)S(1)} %fusion.18, s32[1024]{0:T(1024)S(1)} %fusion.22), kind=kCustom, calls=%fused_computation | custom fusion | bytes 8392704 | tf_op jit(solution)/shard_map/gather | solution.py:32
  45.2 7.2 %gather.9 = bf16[8,32,4,2048]{3,2,1,0:T(4,128)(2,1)} reshape(bf16[1024,2048]{1,0:T(8,128)(2,1)} %gather_fusion) | data formatting | bytes 8388608 | tf_op jit(solution)/shard_map/gather | solution.py:32
  52.4 8.5 %copy_select_fusion = bf16[8,32,4,2048]{3,1,0,2:T(8,128)(2,1)S(1)} fusion(bf16[8,32,4,2048]{3,2,1,0:T(4,128)(2,1)} %gather.9, pred[8,32,4]{1,0,2:T(8,128)(4,1)S(1)} %copy.15), kind=kLoop, calls=%fused_computation.11 | loop fusion | flops 2097152 | bytes 8389632 | tf_op jit(solution)/shard_map/jit(_where)/select_n | solution.py:32
  60.9 57.5 %all_to_all.10 = bf16[32,32,2048]{2,1,0:T(8,128)(2,1)S(1)} all-to-all(bf16[32,32,2048]{2,1,0:T(8,128)(2,1)S(1)} %bitcast.36), channel_id=1, replica_groups=mesh['req'=32,'tp'=4] {'req'}, dimensions={0} | all-to-all | bytes 8388608 | tf_op jit(solution)/shard_map/all_to_all | solution.py:35
  118.4 2.1 copy-done
  120.5 10.2 %fusion.4 = f32[1024,1408]{1,0:T(8,128)} fusion(bf16[1024,2048]{1,0:T(8,128)(2,1)S(1)} %bitcast.38, bf16[1,2048,1408]{2,1,0:T(8,128)(2,1)} %param.13), kind=kOutput, calls=%fused_computation.8 | convolution fusion | flops 5905580032 | bytes 15728640 | tf_op jit(solution)/shard_map/dot_general | solution.py:38
  130.8 20.6 %fusion.10 = bf16[1024,2048]{1,0:T(8,128)(2,1)} fusion(bf16[1,1408,2048]{2,1,0:T(8,128)(2,1)} %param.15, f32[1024,1408]{1,0:T(8,128)} %fusion.4, bf16[1024,2048]{1,0:T(8,128)(2,1)} %bitcast.39, bf16[1,2048,1408]{2,1,0:T(8,128)(2,1)} %param.14), kind=kOutput, calls=%fused_computation.12 | convolution fusion | flops 11821907968 | bytes 25690112 | tf_op jit(solution)/shard_map/dot_general | solution.py:41
  151.4 44.1 %reduce-scatter.2.cloned.1.call-done = bf16[32,32,512]{2,1,0:T(8,128)(2,1)} async-done(((bf16[32,32,2048]{2,1,0:T(8,128)(2,1)}), bf16[32,32,512]{2,1,0:T(8,128)(2,1)}) %reduce-scatter.2.cloned.1.call-update) | async-done | bytes 1048592 | tf_op jit(solution)/shard_map/reduce_scatter | solution.py:43
  195.5 7.2 %all-to-all-start.1 = ((bf16[32,32,512]{2,1,0:T(8,128)(2,1)}), bf16[32,32,512]{2,1,0:T(8,128)(2,1)S(1)}, u32[]{:S(2)}, u32[]{:S(2)}) async-start(bf16[32,32,512]{2,1,0:T(8,128)(2,1)} %reduce-scatter.2.cloned.1.call-done), calls=%async_computation.2 | async-start | bytes 2097152 | tf_op jit(solution)/shard_map/all_to_all | solution.py:49
  202.9 16.6 %all-to-all-done.1 = bf16[32,32,512]{2,1,0:T(8,128)(2,1)S(1)} async-done(((bf16[32,32,512]{2,1,0:T(8,128)(2,1)}), bf16[32,32,512]{2,1,0:T(8,128)(2,1)S(1)}, u32[]{:S(2)}, u32[]{:S(2)}) %all-to-all-start.1) | async-done | bytes 1048608 | tf_op jit(solution)/shard_map/all_to_all | solution.py:49
  219.6 0.8 copy.21
  220.7 2.0 gather_fusion.1
  223.4 1.3 multiply_reduce_fusion
  224.8 8.6 %psum.7 = f32[256]{0:T(256)S(1)} all-reduce(f32[256]{0:T(256)S(1)} %multiply_reduce_fusion.1), channel_id=1, replica_groups=mesh['req'=32,'tp'=4] {'tp'}, use_global_device_ids=true, to_apply=%region_9.10 | all-reduce | flops 256 | bytes 2048 | tf_op jit(solution)/shard_map/psum | solution.py:55
  233.4 0.8 multiply_convert_fusion.1
  (32 shorter events, 2.6 us)
Async XLA Ops:
  7.2 29.0 %all-gather.2.cloned.1.call-start = ((), (), s32[]{:S(2)}) async-start(), calls=%async_computation.3 | async-start | bytes 1310720 | tf_op jit(solution)/shard_map/all_gather | solution.py:19
  7.9 187.6 %reduce-scatter.2.cloned.1.call-start = ((), (), s32[]{:S(2)}) async-start(), calls=%async_computation.4 | async-start | bytes 5242880 | tf_op jit(solution)/shard_map/reduce_scatter | solution.py:43
  118.4 2.1 copy-start
  151.4 51.4 %copy-start.2 = (f32[256,2]{0,1:T(2,128)S(1)}, f32[256,2]{0,1:T(2,128)}, u32[]{:S(2)}) copy-start(f32[256,2]{0,1:T(2,128)} %param.10) | copy-start | bytes 6148
  195.5 24.1 %all-to-all-start.1 = ((bf16[32,32,512]{2,1,0:T(8,128)(2,1)}), bf16[32,32,512]{2,1,0:T(8,128)(2,1)S(1)}, u32[]{:S(2)}, u32[]{:S(2)}) async-start(bf16[32,32,512]{2,1,0:T(8,128)(2,1)} %reduce-scatter.2.cloned.1.call-done), calls=%async_computation.2 | async-start | bytes 2097152 | tf_op jit(solution)/shard_map/all_to_all | solution.py:49
  220.7 4.0 %copy-start.1 = (bf16[256,512]{1,0:T(8,128)(2,1)S(1)}, bf16[256,512]{1,0:T(8,128)(2,1)}, u32[]{:S(2)}) copy-start(bf16[256,512]{1,0:T(8,128)(2,1)} %param.8) | copy-start | bytes 786436
  220.7 12.7 %copy-start.3 = (f32[512]{0:T(512)S(1)}, f32[512]{0:T(512)}, u32[]{:S(2)}) copy-start(f32[512]{0:T(512)} %param.12) | copy-start | bytes 6148
Sparse Core Ops, SparseCore 0:
  9.7 26.4 all-gather.1
  151.5 43.9 reduce-scatter.1
where the time goes:
time: 242 us; the launch traced here: 241 us
  waiting for transfers between devices  80.8 us (33%)
  blocking collectives  66.1 us (27%)
  matrix products  30.9 us (13%)
  local copies, waits for them, and re-layouts  26 us (11%)
  other arithmetic  15.8 us (7%)
  between operations  14.2 us (6%)
  starting transfers between devices  7.31 us (3%)
    all_to_all x1, blocking collectives, shards(): lax.all_to_all(outgoing, 'req', split_axis=0, concat_axis=0, tiled=True)  57.5 us
    reduce_scatter x1, waiting for transfers between devices, shards(): lax.psum_scatter(partial_out.reshape(sources, items, widths).astype(jnp.b...  44.1 us
    dot_general x1, matrix products, shards(): jnp.dot(activ, down_weight[0], preferred_element_type=jnp.float32)  20.6 us
    all_gather x1, waiting for transfers between devices, shards(): lax.all_gather(hidden, 'tp', axis=1, tiled=True).astype(jnp.float32)  19.4 us
    all_to_all x1, waiting for transfers between devices, shards(): lax.all_to_all(summed, 'req', split_axis=0, concat_axis=0, tiled=True)  16.6 us
    gather x2, local copies, waits for them, and re-layouts, shards(): normed_in[slot_row]  13.2 us
    dot_general x1, matrix products, shards(): jnp.dot(flat_rows, gate_weight[0], preferred_element_type=jnp.float32)  10.2 us
    psum x1, blocking collectives, shards(): out_sums = lax.psum(jnp.sum(total_stream * total_stream, axis=1), 'tp')  8.58 us
  transfers between devices with their start and end apart: 3, of which 3 were waited for; matrix products, arithmetic and copies ran while one was open for 4% of the time, Pallas kernels for 0%

commit v1 on v0

--- a/solution.py
+++ b/solution.py
@@ -16,7 +16,24 @@
     copies = req_count // E
     slot_count = CAP // copies
     stream = hidden.astype(jnp.float32)
-    whole_rows = lax.all_gather(hidden, "tp", axis=1, tiled=True).astype(jnp.float32)
+
+    def block_choose(local_block, comm_axis, out_dim):
+        total_devices = lax.axis_size(comm_axis)
+        bank = [(b, (b + 1) % total_devices) for b in range(total_devices)]
+        prior, z = ([local_block], [local_block])
+        chunks = [(b, (b - 1) % total_devices) for b in range(total_devices)]
+        for _ in range(total_devices // 2):
+            prior.append(lax.ppermute(prior[-1], comm_axis, bank))
+        for _ in range((total_devices - 1) // 2):
+            z.append(lax.ppermute(z[-1], comm_axis, chunks))
+        w2 = jnp.concatenate([*prior[::-1], *z[1:]], out_dim)
+        return jnp.roll(
+            w2,
+            (lax.axis_index(comm_axis) - total_devices // 2) * local_block.shape[out_dim],
+            out_dim,
+        )
+
+    whole_rows = block_choose(hidden, "tp", 1).astype(jnp.float32)
     meansq = jnp.sum(whole_rows * whole_rows, axis=1) / full_width
     normed_in = (whole_rows * lax.rsqrt(meansq + epsilon)[:, None] * pre_gain[None, :]).astype(
         jnp.bfloat16

time: 242 us -> 229 us (0.946)
  waiting for transfers between devices: 80.8 us -> 65.2 us
  starting transfers between devices: 7.31 us -> 10.9 us
    all_gather x1 -> x0, waiting for transfers between devices: 19.4 us -> none  [shards(): lax.all_gather(hidden, 'tp', axis=1, tiled=True).astype(jnp.float32)]
    ppermute x0 -> x3, waiting for transfers between devices: none -> 5.83 us  [the longest x2 5.83 us: block_choose(): prior.append(lax.ppermute(prior[-1], comm_axis, bank))]
    ppermute x0 -> x3, starting transfers between devices: none -> 3.61 us  [the longest x2 2.03 us: block_choose(): prior.append(lax.ppermute(prior[-1], comm_axis, bank))]
  transfers between devices with their start and end apart: 3 -> 5, of which waited for: 3 -> 4; matrix products, arithmetic and copies ran while one was open for 4% -> 4% of each run, Pallas kernels for 0% -> 0%
where the time goes in v1:
time: 229 us
  blocking collectives  66.9 us (29%)
  waiting for transfers between devices  65.2 us (28%)
  matrix products  30.9 us (13%)
  local copies, waits for them, and re-layouts  27.1 us (12%)
  between operations  14.3 us (6%)
  other arithmetic  13.4 us (6%)
  starting transfers between devices  10.9 us (5%)
    all_to_all x1, blocking collectives, shards(): lax.all_to_all(outgoing, 'req', split_axis=0, concat_axis=0, tiled=True)  58.4 us
    reduce_scatter x1, waiting for transfers between devices, shards(): lax.psum_scatter(partial_out.reshape(sources, items, widths).astype(jnp.b...  42.7 us
    dot_general x1, matrix products, shards(): jnp.dot(activ, down_weight[0], preferred_element_type=jnp.float32)  20.6 us
    all_to_all x1, waiting for transfers between devices, shards(): lax.all_to_all(summed, 'req', split_axis=0, concat_axis=0, tiled=True)  16.6 us
    gather x2, local copies, waits for them, and re-layouts, shards(): normed_in[slot_row]  13.2 us
    dot_general x1, matrix products, shards(): jnp.dot(flat_rows, gate_weight[0], preferred_element_type=jnp.float32)  10.2 us
    psum x1, blocking collectives, shards(): out_sums = lax.psum(jnp.sum(total_stream * total_stream, axis=1), 'tp')  8.56 us
    select_n x1, other arithmetic, shards(): jnp.where(slot_live[:, None], normed_in[slot_row], jnp.zeros((), jnp.bflo...  8.47 us
  transfers between devices with their start and end apart: 5, of which 4 were waited for; matrix products, arithmetic and copies ran while one was open for 4% of the time, Pallas kernels for 0%

profile of v1, /device:TPU:0, one launch (start us, length us, event | category | flops | bytes accessed | tf_op | source)
XLA Modules:
  0.0 228.6 jit_solution(11939216720685359319)
XLA Ops:
  7.2 1.7 collective-permute-start
  9.0 1.6 collective-permute-start.2
  10.5 0.8 copy.13
  12.3 1.1 reduce-window.6
  14.1 2.8 %collective-permute-done = bf16[256,512]{1,0:T(8,128)(2,1)S(1)} collective-permute-done((bf16[256,512]{1,0:T(8,128)(2,1)}, bf16[256,512]{1,0:T(8,128)(2,1)S(1)}, u32[]{:S(2)}, u32[]{:S(2)}) %collective-permute-start) | collective-permute-done | bytes 262176 | tf_op jit(solution)/shard_map/ppermute | solution.py:26
  17.2 2.4 %scatter_custom_fusion.1 = s32[1024]{0:T(1024)S(1)} fusion(s32[512]{0:T(512)S(1)} %bitcast.42, s32[512]{0:T(512)S(1)} %add_select_fusion, s32[]{:T(128)} %constant.60.clone.1), kind=kCustom, calls=%fused_computation.49 | custom fusion | bytes 4100 | tf_op jit(solution)/shard_map/scatter | solution.py:47
  19.7 2.4 %scatter_custom_fusion = pred[1024]{0:T(1024)(128)(4,1)S(1)} fusion(s32[512]{0:T(512)S(1)} %bitcast.43, pred[512]{0:T(512)(128)(4,1)S(1)} %broadcast.100, pred[]{:T(512)} %constant.58.clone.1), kind=kCustom, calls=%fused_computation.52 | custom fusion | bytes 1025 | tf_op jit(solution)/shard_map/scatter | solution.py:48
  22.4 3.0 %collective-permute-done.1 = bf16[256,512]{1,0:T(8,128)(2,1)S(1)} collective-permute-done((bf16[256,512]{1,0:T(8,128)(2,1)S(1)}, bf16[256,512]{1,0:T(8,128)(2,1)S(1)}, u32[]{:S(2)}, u32[]{:S(2)}) %collective-permute-start.1) | collective-permute-done | bytes 262176 | tf_op jit(solution)/shard_map/ppermute | solution.py:26
  25.5 1.0 constant_dynamic-update-slice_fusion.5
  27.3 6.0 %gather_fusion = bf16[1024,2048]{1,0:T(8,128)(2,1)} fusion(bf16[256,2048]{1,0:T(8,128)(2,1)S(1)} %fusion.18, s32[1024]{0:T(1024)S(1)} %fusion.22), kind=kCustom, calls=%fused_computation | custom fusion | bytes 8392704 | tf_op jit(solution)/shard_map/gather | solution.py:49
  33.3 7.2 %gather.9 = bf16[8,32,4,2048]{3,2,1,0:T(4,128)(2,1)} reshape(bf16[1024,2048]{1,0:T(8,128)(2,1)} %gather_fusion) | data formatting | bytes 8388608 | tf_op jit(solution)/shard_map/gather | solution.py:49
  40.5 8.5 %copy_select_fusion = bf16[8,32,4,2048]{3,1,0,2:T(8,128)(2,1)S(1)} fusion(bf16[8,32,4,2048]{3,2,1,0:T(4,128)(2,1)} %gather.9, pred[8,32,4]{1,0,2:T(8,128)(4,1)S(1)} %copy.15), kind=kLoop, calls=%fused_computation.11 | loop fusion | flops 2097152 | bytes 8389632 | tf_op jit(solution)/shard_map/jit(_where)/select_n | solution.py:49
  49.0 58.4 %all_to_all.10 = bf16[32,32,2048]{2,1,0:T(8,128)(2,1)S(1)} all-to-all(bf16[32,32,2048]{2,1,0:T(8,128)(2,1)S(1)} %bitcast.36), channel_id=1, replica_groups=mesh['req'=32,'tp'=4] {'req'}, dimensions={0} | all-to-all | bytes 8388608 | tf_op jit(solution)/shard_map/all_to_all | solution.py:52
  107.4 2.1 copy-done
  109.5 10.2 %fusion.4 = f32[1024,1408]{1,0:T(8,128)} fusion(bf16[1024,2048]{1,0:T(8,128)(2,1)S(1)} %bitcast.38, bf16[1,2048,1408]{2,1,0:T(8,128)(2,1)} %param.13), kind=kOutput, calls=%fused_computation.8 | convolution fusion | flops 5905580032 | bytes 15728640 | tf_op jit(solution)/shard_map/dot_general | solution.py:55
  119.7 20.6 %fusion.10 = bf16[1024,2048]{1,0:T(8,128)(2,1)} fusion(bf16[1,1408,2048]{2,1,0:T(8,128)(2,1)} %param.15, f32[1024,1408]{1,0:T(8,128)} %fusion.4, bf16[1024,2048]{1,0:T(8,128)(2,1)} %bitcast.39, bf16[1,2048,1408]{2,1,0:T(8,128)(2,1)} %param.14), kind=kOutput, calls=%fused_computation.12 | convolution fusion | flops 11821907968 | bytes 25690112 | tf_op jit(solution)/shard_map/dot_general | solution.py:58
  140.4 42.7 %reduce-scatter.2.cloned.1.call-done = bf16[32,32,512]{2,1,0:T(8,128)(2,1)} async-done(((bf16[32,32,2048]{2,1,0:T(8,128)(2,1)}), bf16[32,32,512]{2,1,0:T(8,128)(2,1)}) %reduce-scatter.2.cloned.1.call-update) | async-done | bytes 1048592 | tf_op jit(solution)/shard_map/reduce_scatter | solution.py:60
  183.1 7.2 %all-to-all-start.1 = ((bf16[32,32,512]{2,1,0:T(8,128)(2,1)}), bf16[32,32,512]{2,1,0:T(8,128)(2,1)S(1)}, u32[]{:S(2)}, u32[]{:S(2)}) async-start(bf16[32,32,512]{2,1,0:T(8,128)(2,1)} %reduce-scatter.2.cloned.1.call-done), calls=%async_computation.2 | async-start | bytes 2097152 | tf_op jit(solution)/shard_map/all_to_all | solution.py:66
  190.5 16.6 %all-to-all-done.1 = bf16[32,32,512]{2,1,0:T(8,128)(2,1)S(1)} async-done(((bf16[32,32,512]{2,1,0:T(8,128)(2,1)}), bf16[32,32,512]{2,1,0:T(8,128)(2,1)S(1)}, u32[]{:S(2)}, u32[]{:S(2)}) %all-to-all-start.1) | async-done | bytes 1048608 | tf_op jit(solution)/shard_map/all_to_all | solution.py:66
  207.1 0.8 copy.21
  208.3 2.0 gather_fusion.1
  210.9 1.3 multiply_reduce_fusion
  212.4 8.6 %psum.7 = f32[256]{0:T(256)S(1)} all-reduce(f32[256]{0:T(256)S(1)} %multiply_reduce_fusion.1), channel_id=1, replica_groups=mesh['req'=32,'tp'=4] {'tp'}, use_global_device_ids=true, to_apply=%region_9.10 | all-reduce | flops 256 | bytes 2048 | tf_op jit(solution)/shard_map/psum | solution.py:72
  220.9 0.8 multiply_convert_fusion.1
  (45 shorter events, 4.3 us)
Async XLA Ops:
  7.2 19.5 %copy-start.1 = (bf16[256,512]{1,0:T(8,128)(2,1)S(1)}, bf16[256,512]{1,0:T(8,128)(2,1)}, u32[]{:S(2)}) copy-start(bf16[256,512]{1,0:T(8,128)(2,1)} %param.8) | copy-start | bytes 786436
  7.2 19.8 %copy-start.2 = (f32[2048]{0:T(1024)S(1)}, f32[2048]{0:T(1024)}, u32[]{:S(2)}) copy-start(f32[2048]{0:T(1024)} %param.11) | copy-start | bytes 24580
  7.2 175.9 %reduce-scatter.2.cloned.1.call-start = ((), (), s32[]{:S(2)}) async-start(), calls=%async_computation.3 | async-start | bytes 5242880 | tf_op jit(solution)/shard_map/reduce_scatter | solution.py:60
  7.2 9.7 %collective-permute-start = (bf16[256,512]{1,0:T(8,128)(2,1)}, bf16[256,512]{1,0:T(8,128)(2,1)S(1)}, u32[]{:S(2)}, u32[]{:S(2)}) collective-permute-start(bf16[256,512]{1,0:T(8,128)(2,1)} %param.8), channel_id=1, source_target_pairs={{0,1},{1,2},{2,3},{3,0},{4,5},{5,6},{6,7},{7,4},{8,9},{9,10},{10,1... | collective-permute-start | bytes 786440 | tf_op jit(solution)/shard_map/ppermute | solution.py:26
  9.0 17.6 %collective-permute-start.2 = (bf16[256,512]{1,0:T(8,128)(2,1)}, bf16[256,512]{1,0:T(8,128)(2,1)S(1)}, u32[]{:S(2)}, u32[]{:S(2)}) collective-permute-start(bf16[256,512]{1,0:T(8,128)(2,1)} %param.8), channel_id=1, source_target_pairs={{0,3},{1,0},{2,1},{3,2},{4,7},{5,4},{6,5},{7,6},{8,11},{9,8},{10,9... | collective-permute-start | bytes 786440 | tf_op jit(solution)/shard_map/ppermute | solution.py:28
  16.9 8.6 %collective-permute-start.1 = (bf16[256,512]{1,0:T(8,128)(2,1)S(1)}, bf16[256,512]{1,0:T(8,128)(2,1)S(1)}, u32[]{:S(2)}, u32[]{:S(2)}) collective-permute-start(bf16[256,512]{1,0:T(8,128)(2,1)S(1)} %collective-permute-done), channel_id=1, source_target_pairs={{0,1},{1,2},{2,3},{3,0},{4,5},{5,6},{6,7},{7,4},{8,9},{9,10},{10,1... | collective-permute-start | bytes 786440 | tf_op jit(solution)/shard_map/ppermute | solution.py:26
  107.4 2.1 copy-start
  140.3 50.0 %copy-start.3 = (f32[256,2]{0,1:T(2,128)S(1)}, f32[256,2]{0,1:T(2,128)}, u32[]{:S(2)}) copy-start(f32[256,2]{0,1:T(2,128)} %param.10) | copy-start | bytes 6148
  183.1 24.1 %all-to-all-start.1 = ((bf16[32,32,512]{2,1,0:T(8,128)(2,1)}), bf16[32,32,512]{2,1,0:T(8,128)(2,1)S(1)}, u32[]{:S(2)}, u32[]{:S(2)}) async-start(bf16[32,32,512]{2,1,0:T(8,128)(2,1)} %reduce-scatter.2.cloned.1.call-done), calls=%async_computation.2 | async-start | bytes 2097152 | tf_op jit(solution)/shard_map/all_to_all | solution.py:66
  208.2 12.7 %copy-start.4 = (f32[512]{0:T(512)S(1)}, f32[512]{0:T(512)}, u32[]{:S(2)}) copy-start(f32[512]{0:T(512)} %param.12) | copy-start | bytes 6148
Sparse Core Ops, SparseCore 0:
  140.5 42.5 reduce-scatter.1
